TPU v7x, 512 devices: a whole 4x8x8 slice. The times are simulated.
512 devices in a mesh: seq: 64 (over z, x, core), head: 8 (over y).
Axes of the slice: x: 4, y: 8, z: 8, core: 2. Of those that a mesh axis runs over, the one named last changes fastest.
Arguments:
- projected: float32 [65536, 2560], P(('seq', 'head')), may hold values from -6 to 6
- out_grads: float32 [65536, 2048], P(('seq', 'head')), may hold values from -6 to 6
- conv_weight: float32 [3, 2560], replicated, may hold values from -2.4 to 2.4
- doc_lengths: int32 [16], replicated, may hold values from 1 to 32768, 65536 in all
Outputs:
- grad_projected: float32 [65536, 2560], P(('seq', 'head'))
- grad_conv: float32 [3, 2560], replicated
Inputs may be any that keep to these rules, and one draw needn't show every extreme that they name: `doc_lengths`: the 16 documents fill the 65536 tokens end to end; the longest holds exactly half of 65536 tokens.
All inputs are finite; a program needn't handle non-finite values.
Results may differ from a plain program's by a relative error of at most 0.0003.
Values sent between devices are 32-bit elements; how exact they have to be, the bound alone decides.
No kernel may reach another device: no remote copies, remote signals or barrier semaphores. Data moves between devices by JAX's collectives and lax.ppermute only.
A program may use at most 128 MiB of HBM per device.

v0:
```python
import math
import jax
import jax.numpy as jnp
import numpy as np
from jax import lax
from jax.sharding import PartitionSpec as P

KEY_DIM = 16
HEAD_DIM = 128
HIGHEST = lax.Precision.HIGHEST


def segment_sum(gathered, flags, here, reverse):
    count = gathered.shape[0]
    index = jnp.arange(count, dtype=jnp.int32)
    started = flags > 0.5
    if reverse:
        bound = jnp.min(jnp.where((index > here) & started, index, count - 1))
        take = (index > here) & (index <= bound)
    else:
        bound = jnp.max(jnp.where((index < here) & started, index, 0))
        take = (index >= bound) & (index < here)
    return jnp.sum(jnp.where(take[:, None], gathered, 0.0), axis=0)


def carried_in(state, norm, extra, flags, axis, reverse):
    here = lax.axis_index(axis)
    size = state.size
    packed = jnp.concatenate([state.reshape(-1), norm.reshape(-1), extra])
    width = 128
    padded = jnp.pad(packed, (0, -packed.shape[0] % width)).reshape(-1, width)
    gathered = lax.all_gather(padded, axis).reshape(lax.axis_size(axis), -1)
    if flags is None:
        flags = gathered[:, packed.shape[0] - 1]
    total = segment_sum(gathered[:, : size + norm.size], flags, here, reverse)
    return (total[:size].reshape(state.shape), total[size:].reshape(norm.shape), flags)


def passed_along(value, axis, steps):
    count = lax.axis_size(axis)
    initial, last = (max(0, -steps), min(count, count - steps))
    return lax.ppermute(value, axis, [(source, source + steps) for source in range(initial, last)])


def feature_map(columns):
    key_size = columns.shape[1]
    upper_i, upper_j = np.triu_indices(key_size)
    factors = np.where(upper_i == upper_j, 1.0 / math.sqrt(2.0), 1.0).astype(np.float32)
    products = columns[:, upper_i, :] * columns[:, upper_j, :] * jnp.asarray(factors)[None, :, None]
    constant = jnp.ones((columns.shape[0], 1, columns.shape[2]), jnp.float32)
    return jnp.concatenate([constant, columns, products], axis=1)


def doc_place(doc_lengths, anchor, amount):
    positions = anchor + jnp.arange(amount, dtype=jnp.int32)
    starts = jnp.cumsum(doc_lengths) - doc_lengths
    begins = jnp.max(jnp.where(starts[None, :] <= positions[:, None], starts[None, :], 0), axis=1)
    return (begins, positions - begins)


def conv_forward(signal, leading, weights, offsets):
    row_count = signal.shape[0]
    behind = jnp.concatenate([leading, signal], axis=0)
    back_one = behind[1 : row_count + 1] * (offsets[0:row_count] >= 1).astype(jnp.float32)[:, None]
    back_two = behind[0:row_count] * (offsets[0:row_count] >= 2).astype(jnp.float32)[:, None]
    return weights[0] * signal + weights[1] * back_one + weights[2] * back_two


def conv_backward(grad_rows, trailing, signal, leading, weights, offsets):
    row_count = grad_rows.shape[0]
    ahead_rows = jnp.concatenate([grad_rows, trailing], axis=0)
    ahead_one = (
        ahead_rows[1 : row_count + 1]
        * (offsets[1 : row_count + 1] >= 1).astype(jnp.float32)[:, None]
    )
    ahead_two = (
        ahead_rows[2 : row_count + 2]
        * (offsets[2 : row_count + 2] >= 2).astype(jnp.float32)[:, None]
    )
    grad_signal = weights[0] * grad_rows + weights[1] * ahead_one + weights[2] * ahead_two
    behind = jnp.concatenate([leading, signal], axis=0)
    own_one = (offsets[0:row_count] >= 1).astype(jnp.float32)[:, None]
    own_two = (offsets[0:row_count] >= 2).astype(jnp.float32)[:, None]
    grad_weights = jnp.stack(
        [
            jnp.sum(grad_rows * signal, axis=0),
            jnp.sum(grad_rows * behind[1 : row_count + 1] * own_one, axis=0),
            jnp.sum(grad_rows * behind[0:row_count] * own_two, axis=0),
        ],
        axis=0,
    )
    return (grad_signal, grad_weights)


def attention_grads(mixed_rows, out_flat, begins, stretch_start):
    length = mixed_rows.shape[0]
    head_width = 2 * KEY_DIM + HEAD_DIM
    local_heads = mixed_rows.shape[1] // head_width
    block_len = min(128, length)
    blocks = length // block_len
    scale_key = KEY_DIM ** (-0.25)
    shaped = mixed_rows.reshape(length, local_heads, head_width)
    query_cols = jnp.transpose(shaped[:, :, :KEY_DIM], (1, 2, 0)) * scale_key
    key_cols = jnp.transpose(shaped[:, :, KEY_DIM : 2 * KEY_DIM], (1, 2, 0)) * scale_key
    values = shaped[:, :, 2 * KEY_DIM :]
    upstream = out_flat.reshape(length, local_heads, HEAD_DIM)
    query_feat, query_pull = jax.vjp(feature_map, query_cols)
    key_feat, key_pull = jax.vjp(feature_map, key_cols)
    feat_count = query_feat.shape[1]
    last_begin = begins[length - 1]
    has_start = (last_begin >= stretch_start).astype(jnp.float32).reshape(1)
    tail_mask = (begins == last_begin).astype(jnp.float32)
    tail_feat = key_feat * tail_mask[None, None, :]
    tail_state = jnp.einsum("hfl,lhe->hfe", tail_feat, values, precision=HIGHEST)
    tail_norm = jnp.sum(tail_feat, axis=2)
    prefix = carried_in(tail_state, tail_norm, has_start, None, "seq", False)
    flags = prefix[2]
    causal = jnp.arange(block_len)[:, None] >= jnp.arange(block_len)[None, :]
    indices = jnp.arange(blocks, dtype=jnp.int32)

    def forward_block(carried, block_index):
        carry_state, carry_norm = carried
        offset_rows = block_index * block_len
        block_start = stretch_start + offset_rows
        query_blk = lax.dynamic_slice_in_dim(query_feat, offset_rows, block_len, 2)
        key_blk = lax.dynamic_slice_in_dim(key_feat, offset_rows, block_len, 2)
        value_blk = lax.dynamic_slice_in_dim(values, offset_rows, block_len, 0)
        doc_blk = lax.dynamic_slice_in_dim(begins, offset_rows, block_len, 0)
        allowed = causal & (doc_blk[:, None] == doc_blk[None, :])
        scores = jnp.where(
            allowed[None], jnp.einsum("hft,hfs->hts", query_blk, key_blk, precision=HIGHEST), 0.0
        )
        from_carry = (doc_blk < block_start).astype(jnp.float32)
        numerator = jnp.einsum("hts,she->the", scores, value_blk, precision=HIGHEST) + from_carry[
            :, None, None
        ] * jnp.einsum("hft,hfe->the", query_blk, carry_state, precision=HIGHEST)
        denominator = jnp.sum(scores, axis=2) + from_carry[None, :] * jnp.einsum(
            "hft,hf->ht", query_blk, carry_norm, precision=HIGHEST
        )
        block_tail = (doc_blk == doc_blk[block_len - 1]).astype(jnp.float32)
        carry_keep = (doc_blk[block_len - 1] < block_start).astype(jnp.float32)
        tail_keys = key_blk * block_tail[None, None, :]
        next_state = (
            jnp.einsum("hfs,she->hfe", tail_keys, value_blk, precision=HIGHEST)
            + carry_keep * carry_state
        )
        next_norm = jnp.sum(tail_keys, axis=2) + carry_keep * carry_norm
        return ((next_state, next_norm), (numerator, denominator, carry_state, carry_norm, scores))

    forward_out = lax.scan(forward_block, (prefix[0], prefix[1]), indices)
    numerators, denominators, states, norms, kept_scores = forward_out[1]
    denom_rows = jnp.transpose(denominators, (0, 2, 1)).reshape(length, local_heads)
    attended = numerators.reshape(length, local_heads, HEAD_DIM) / denom_rows[:, :, None]
    grad_num = upstream / denom_rows[:, :, None]
    scalar_grad = -jnp.sum(upstream * attended, axis=2) / denom_rows
    lead_mask = (begins < stretch_start).astype(jnp.float32)
    lead_feat = query_feat * lead_mask[None, None, :]
    lead_state = jnp.einsum("hfl,lhe->hfe", lead_feat, grad_num, precision=HIGHEST)
    lead_norm = jnp.einsum("hfl,lh->hf", lead_feat, scalar_grad, precision=HIGHEST)
    suffix = carried_in(lead_state, lead_norm, jnp.zeros((0,), jnp.float32), flags, "seq", True)

    def backward_block(carried, inputs):
        back_state, back_norm = carried
        block_index, carry_state, carry_norm, scores = inputs
        offset_rows = block_index * block_len
        block_start = stretch_start + offset_rows
        query_blk = lax.dynamic_slice_in_dim(query_feat, offset_rows, block_len, 2)
        key_blk = lax.dynamic_slice_in_dim(key_feat, offset_rows, block_len, 2)
        value_blk = lax.dynamic_slice_in_dim(values, offset_rows, block_len, 0)
        doc_blk = lax.dynamic_slice_in_dim(begins, offset_rows, block_len, 0)
        grad_blk = lax.dynamic_slice_in_dim(grad_num, offset_rows, block_len, 0)
        scalar_blk = lax.dynamic_slice_in_dim(scalar_grad, offset_rows, block_len, 0)
        scalar_cols = scalar_blk.T
        allowed = causal & (doc_blk[:, None] == doc_blk[None, :])
        dscores = jnp.where(
            allowed[None],
            jnp.einsum("the,she->hts", grad_blk, value_blk, precision=HIGHEST)
            + scalar_cols[:, :, None],
            0.0,
        )
        from_carry = (doc_blk < block_start).astype(jnp.float32)
        block_tail = (doc_blk == doc_blk[block_len - 1]).astype(jnp.float32)
        carry_keep = (doc_blk[block_len - 1] < block_start).astype(jnp.float32)
        grad_query = jnp.einsum("hts,hfs->hft", dscores, key_blk, precision=HIGHEST) + from_carry[
            None, None, :
        ] * (
            jnp.einsum("hfe,the->hft", carry_state, grad_blk, precision=HIGHEST)
            + carry_norm[:, :, None] * scalar_cols[:, None, :]
        )
        grad_key = jnp.einsum("hts,hft->hfs", dscores, query_blk, precision=HIGHEST) + block_tail[
            None, None, :
        ] * (
            jnp.einsum("hfe,she->hfs", back_state, value_blk, precision=HIGHEST)
            + back_norm[:, :, None]
        )
        grad_value = jnp.einsum("hts,the->she", scores, grad_blk, precision=HIGHEST) + block_tail[
            :, None, None
        ] * jnp.einsum("hfs,hfe->she", key_blk, back_state, precision=HIGHEST)
        lead_blk = query_blk * from_carry[None, None, :]
        next_state = (
            jnp.einsum("hft,the->hfe", lead_blk, grad_blk, precision=HIGHEST)
            + carry_keep * back_state
        )
        next_norm = (
            jnp.einsum("hft,th->hf", lead_blk, scalar_blk, precision=HIGHEST)
            + carry_keep * back_norm
        )
        return ((next_state, next_norm), (grad_query, grad_key, grad_value))

    swept_back = lax.scan(
        backward_block, (suffix[0], suffix[1]), (indices, states, norms, kept_scores), reverse=True
    )
    grad_qblocks, grad_kblocks, grad_vblocks = swept_back[1]
    query_grad = jnp.transpose(grad_qblocks, (1, 2, 0, 3)).reshape(local_heads, feat_count, length)
    key_grad = jnp.transpose(grad_kblocks, (1, 2, 0, 3)).reshape(local_heads, feat_count, length)
    value_grad = grad_vblocks.reshape(length, local_heads, HEAD_DIM)
    query_in = jnp.transpose(query_pull(query_grad)[0] * scale_key, (2, 0, 1))
    key_in = jnp.transpose(key_pull(key_grad)[0] * scale_key, (2, 0, 1))
    return jnp.concatenate([query_in, key_in, value_grad], axis=2).reshape(
        length, local_heads * head_width
    )


def on_device(projected, out_grads, conv_weight, doc_lengths):
    row_count = projected.shape[0]
    head_count = lax.axis_size("head")
    seq_index = lax.axis_index("seq")
    head_index = lax.axis_index("head")
    group_len = row_count * head_count
    token_base = (seq_index * head_count + head_index) * row_count
    stretch_start = seq_index * group_len
    token_begins, token_offsets = doc_place(doc_lengths, token_base, row_count + 2)
    leading = passed_along(projected[row_count - 2 :], ("seq", "head"), 1)
    outgoing = conv_forward(projected, leading, conv_weight, token_offsets)
    arrived, upstream = (
        lax.all_to_all(outgoing, "head", split_axis=1, concat_axis=0, tiled=True),
        lax.all_to_all(out_grads, "head", split_axis=1, concat_axis=0, tiled=True),
    )
    group_begins, group_offsets = doc_place(doc_lengths, stretch_start, group_len + 2)
    grad_mixed = attention_grads(arrived, upstream, group_begins[:group_len], stretch_start)
    returned = lax.all_to_all(grad_mixed, "head", split_axis=0, concat_axis=1, tiled=True)
    trailing = passed_along(returned[:2], ("seq", "head"), -1)
    grad_projected, weight_part = conv_backward(
        returned, trailing, projected, leading, conv_weight, token_offsets
    )
    grad_conv = lax.psum(weight_part, ("seq", "head"))
    return (grad_projected, grad_conv)


def solution(mesh):
    return jax.shard_map(
        on_device,
        mesh=mesh,
        in_specs=(P(("seq", "head"), None), P(("seq", "head"), None), P(), P()),
        out_specs=(P(("seq", "head"), None), P()),
        check_vma=False,
    )
```

profile of v0, /device:TPU:1, one launch (start us, length us, event | category | flops | bytes accessed | tf_op | source)
XLA Modules:
  0.0 737.0 jit_solution(17403635177316418319)
XLA Ops:
  8.1 4.0 collective-permute-start
  17.0 3.1 multiply_add_fusion.1
  20.1 6.1 all-to-all-start
  28.1 32.9 %all-to-all-done = f32[128,8,320]{0,2,1:T(8,128)S(1)} async-done(((f32[128,8,320]{0,2,1:T(8,128)}), f32[128,8,320]{0,2,1:T(8,128)S(1)}, u32[]{:S(2)}, u32[]{:S(2)}) %all-to-all-start) | async-done | bytes 1310752 | tf_op jit(solution)/shard_map/all_to_all | solution.py:236
  65.0 3.0 gather_fusion
  68.1 3.1 gather_fusion.1
  71.1 3.0 gather_fusion.2
  74.2 3.0 gather_fusion.3
  77.2 3.4 fusion.89
  80.6 4.3 fusion.98
  88.8 3.6 all-to-all-start.1
  92.7 28.9 %all-to-all-done.1 = f32[128,8,256]{0,2,1:T(8,128)S(1)} async-done(((f32[128,8,256]{0,2,1:T(8,128)}), f32[128,8,256]{0,2,1:T(8,128)S(1)}, u32[]{:S(2)}, u32[]{:S(2)}) %all-to-all-start.1) | async-done | bytes 1048608 | tf_op jit(solution)/shard_map/all_to_all | solution.py:237
  123.2 2.4 reshape.233
  128.4 2.5 copy.272
  131.0 48.2 %all-gather.3.cloned.1.call-done = f32[64,309,128]{2,1,0:T(8,128)} async-done(((f32[1,309,128]{2,1,0:T(8,128)}), f32[64,309,128]{2,1,0:T(8,128)}) %all-gather.3.cloned.1.call-update) | async-done | bytes 10125328 | tf_op jit(solution)/shard_map/all_gather | solution.py:32
  179.2 5.7 copy.305
  188.8 110.3 %while.46 = (s32[]{:T(128)}, f32[2,153,128]{2,1,0:T(8,128)S(1)}, f32[2,153]{1,0:T(2,128)S(1)}, f32[8,128,2,128]{1,0,3,2:T(8,128)}, f32[8,2,128]{2,1,0:T(2,128)S(...) while((s32[]{:T(128)}, f32[2,153,128]{2,1,0:T(8,128)S(1)}, ...), condition=%wide.region_10.11_spmd.clone, body=%wide.region_7.10_spmd.clone.sunk | while | flops 231664960 | bytes 3280461 | solution.py:150
  192.8 4.8 dynamic_update_slice.74
  206.6 4.8 dynamic_update_slice.74
  220.4 4.8 dynamic_update_slice.74
  234.2 4.8 dynamic_update_slice.74
  248.0 4.8 dynamic_update_slice.74
  261.8 4.8 dynamic_update_slice.74
  275.6 4.8 dynamic_update_slice.74
  289.3 4.8 dynamic_update_slice.74
  299.0 2.4 reshape.237
  306.0 2.8 fusion.81
  310.3 88.0 %all-gather.5.cloned.1.call-done = f32[64,309,128]{2,1,0:T(8,128)} async-done(((f32[1,309,128]{2,1,0:T(8,128)}), f32[64,309,128]{2,1,0:T(8,128)}) %all-gather.5.cloned.1.call-update) | async-done | bytes 10125328 | tf_op jit(solution)/shard_map/all_gather | solution.py:32
  398.3 5.7 copy.304
  408.5 112.2 %while.47 = (s32[]{:T(128)}, f32[2,153,128]{2,1,0:T(8,128)S(1)}, f32[2,153]{1,0:T(2,128)S(1)}, f32[8,2,153,128]{3,2,1,0:T(8,128)}, f32[8,2,153,128]{3,2,1,0:T(8,...) while((s32[]{:T(128)}, f32[2,153,128]{2,1,0:T(8,128)S(1)}, ...), condition=%wide.region_14.15_spmd.clone, body=%wide.region_13.14_spmd.clone.sunk | while | flops 462717824 | bytes 4866477 | solution.py:210
  415.4 2.0 fusion.190
  443.4 2.0 fusion.190
  457.4 2.0 fusion.190
  485.4 2.0 fusion.190
  499.4 2.0 fusion.190
  513.4 2.0 fusion.190
  520.8 2.0 copy.242
  526.3 2.0 reshape.243
  529.4 6.0 fusion.85
  535.3 14.0 %scatter_fusion = f32[2,16,1024]{2,0,1:T(2,128)S(1)} fusion(f32[2,16,1024]{2,0,1:T(2,128)S(1)} %split.16, s32[136]{0:T(256)S(1)} %copy-done.16, f32[136,2,1024]{2,1,0:T(2,128)} %get-tuple-element.822), kind=kCustom, calls=%fused_computation.4 | custom fusion | flops 278528 | bytes 3342880 | tf_op jit(solution)/shard_map/transpose(jvp())/scatter-add | solution.py:49
  549.4 7.6 %scatter_fusion.1 = f32[2,16,1024]{2,0,1:T(2,128)S(1)} fusion(f32[2,16,1024]{2,0,1:T(2,128)S(1)} %broadcast.144.clone.1, s32[136]{0:T(256)S(1)} %copy-done.17, f32[136,2,1024]{2,1,0:T(2,128)S(1)} %copy-done.13), kind=kCustom, calls=%fused_computation.5 | custom fusion | flops 278528 | bytes 3342880 | tf_op jit(solution)/shard_map/transpose(jvp())/scatter-add | solution.py:49
  558.4 7.6 %scatter_fusion.3 = f32[2,16,1024]{2,0,1:T(2,128)S(1)} fusion(f32[2,16,1024]{2,0,1:T(2,128)S(1)} %broadcast.144.clone, s32[136]{0:T(256)S(1)} %copy-done.17, f32[136,2,1024]{2,1,0:T(2,128)S(1)} %copy-done.12), kind=kCustom, calls=%fused_computation.7 | custom fusion | flops 278528 | bytes 3342880 | tf_op jit(solution)/shard_map/transpose(jvp())/scatter-add | solution.py:49
  566.0 7.3 scatter_fusion.2
  574.8 3.0 pad_maximum_fusion
  581.3 41.0 %all_to_all.51 = f32[8,128,320]{1,2,0:T(8,128)S(1)} all-to-all(f32[8,128,320]{1,2,0:T(8,128)S(1)} %copy.248), channel_id=1, replica_groups=mesh['seq'=64,'head'=8] {'head'}, dimensions={0} | all-to-all | bytes 2621440 | tf_op jit(solution)/shard_map/all_to_all | solution.py:241
  622.3 2.1 multiply_reduce_fusion.2
  626.8 95.7 %psum.7 = f32[3,2560]{1,0:T(4,128)} all-reduce(f32[3,2560]{1,0:T(4,128)S(1)} %pad_maximum_fusion.5), channel_id=1, replica_groups=mesh['seq'=64,'head'=8] {'seq','head'}, use_global_device_ids=true, to_apply=%region_22.23 | all-reduce | flops 7680 | bytes 61440 | tf_op jit(solution)/shard_map/psum | solution.py:246
  724.1 4.3 fusion.75
  (413 shorter events, 200.4 us)
Async XLA Ops:
  8.1 8.5 %collective-permute-start = (f32[2,2560]{1,0:T(2,128)S(1)}, f32[2,2560]{1,0:T(2,128)S(1)}, u32[]{:S(2)}, u32[]{:S(2)}) collective-permute-start(f32[2,2560]{1,0:T(2,128)S(1)} %slice.116), channel_id=1, source_target_pairs={{0,1},{1,2},{2,3},{3,4},{4,5},{5,6},{6,7},{7,8},{8,9},{9,10},{10,1... | collective-permute-start | bytes 61448 | tf_op jit(solution)/shard_map/ppermute | solution.py:42
  16.6 3.5 copy-start.3
  17.0 3.1 copy-start.5
  20.1 7.4 %copy-start.17 = (s32[136]{0:T(256)S(1)}, s32[136]{0:T(256)}, u32[]{:S(2)}) copy-start(s32[136]{0:T(256)} %constant.158) | copy-start | bytes 1636
  20.1 7.4 %copy-start.16 = (s32[136]{0:T(256)S(1)}, s32[136]{0:T(256)}, u32[]{:S(2)}) copy-start(s32[136]{0:T(256)} %constant.159) | copy-start | bytes 1636
  20.1 40.9 %all-to-all-start = ((f32[128,8,320]{0,2,1:T(8,128)}), f32[128,8,320]{0,2,1:T(8,128)S(1)}, u32[]{:S(2)}, u32[]{:S(2)}) async-start(f32[128,8,320]{0,2,1:T(8,128)} %bitcast.248), calls=%async_computation | async-start | bytes 2621440 | tf_op jit(solution)/shard_map/all_to_all | solution.py:236
  26.2 153.0 %all-gather.3.cloned.1.call-start = ((), (), s32[]{:S(2)}) async-start(), calls=%async_computation.3 | async-start | bytes 10383360 | tf_op jit(solution)/shard_map/all_gather | solution.py:32
  26.3 66.3 %copy-start.15 = (s32[1026]{0:T(1024)}, s32[1026]{0:T(1024)S(1)}, u32[]{:S(2)}) copy-start(s32[1026]{0:T(1024)S(1)} %select_reduce_fusion) | copy-start | bytes 12316
  74.2 3.0 copy-start.18
  84.9 2.6 copy-start.14
  88.8 32.7 %all-to-all-start.1 = ((f32[128,8,256]{0,2,1:T(8,128)}), f32[128,8,256]{0,2,1:T(8,128)S(1)}, u32[]{:S(2)}, u32[]{:S(2)}) async-start(f32[128,8,256]{0,2,1:T(8,128)} %bitcast.256), calls=%async_computation.1 | async-start | bytes 2097152 | tf_op jit(solution)/shard_map/all_to_all | solution.py:237
  92.4 305.8 %all-gather.5.cloned.1.call-start = ((), (), s32[]{:S(2)}) async-start(), calls=%async_computation.4 | async-start | bytes 10383360 | tf_op jit(solution)/shard_map/all_gather | solution.py:32
  125.5 1.7 copy-start.10
  126.6 1.4 copy-start.9
  187.4 1.3 slice-start.1
  301.4 2.9 copy-start.2
  303.3 1.0 copy-start
  522.8 1.7 copy-start.8
  526.3 3.1 copy-start.7
  528.3 7.1 copy-start.1
  535.3 14.0 %copy-start.13 = (f32[136,2,1024]{2,1,0:T(2,128)S(1)}, f32[136,2,1024]{2,1,0:T(2,128)}, u32[]{:S(2)}) copy-start(f32[136,2,1024]{2,1,0:T(2,128)} %get-tuple-element.821) | copy-start | bytes 3342340
  557.0 1.4 copy-start.12
  558.4 7.6 %slice-start = ((f32[2,153,1024]{2,0,1:T(2,128)}), f32[2,16,1024]{2,0,1:T(2,128)S(1)}, s32[]{:S(2)}) async-start(f32[2,153,1024]{2,0,1:T(2,128)} %copy-done.1), calls=%async_computation.5 | async-start | bytes 262144 | tf_op jit(solution)/shard_map/transpose(jvp())/split | solution.py:51
  558.4 7.6 %copy-start.11 = (f32[136,2,1024]{2,1,0:T(2,128)S(1)}, f32[136,2,1024]{2,1,0:T(2,128)}, u32[]{:S(2)}) copy-start(f32[136,2,1024]{2,1,0:T(2,128)} %get-tuple-element.833) | copy-start | bytes 3342340
  581.3 41.0 %copy-start.4 = (f32[128,2560]{0,1:T(8,128)S(1)}, f32[128,2560]{0,1:T(8,128)}, u32[]{:S(2)}) copy-start(f32[128,2560]{0,1:T(8,128)} %copy-done.3) | copy-start | bytes 3932164
  581.3 41.0 %copy-start.6 = (f32[2,2560]{0,1:T(8,128)S(1)}, f32[2,2560]{0,1:T(8,128)}, u32[]{:S(2)}) copy-start(f32[2,2560]{0,1:T(8,128)} %copy-done.5) | copy-start | bytes 61444
  624.9 97.7 %collective-permute-start.1 = (f32[2,2560]{1,0:T(2,128)S(1)}, f32[2,2560]{1,0:T(2,128)S(1)}, u32[]{:S(2)}, u32[]{:S(2)}) collective-permute-start(f32[2,2560]{1,0:T(2,128)S(1)} %copy.249), channel_id=1, source_target_pairs={{1,0},{2,1},{3,2},{4,3},{5,4},{6,5},{7,6},{8,7},{9,8},{10,9},{11,1... | collective-permute-start | bytes 61448 | tf_op jit(solution)/shard_map/ppermute | solution.py:42
Sparse Core Ops, SparseCore 0:
  87.6 91.5 all-gather.2
  309.7 88.5 all-gather.4
where the time goes:
time: 743 us; the launch traced here: 737 us
  waiting for transfers between devices  198 us (27%)
  local copies, waits for them, and re-layouts  146 us (20%)
  blocking collectives  137 us (18%)
  matrix products  117 us (16%)
  other arithmetic  85.8 us (12%)
  loops' own time  22.4 us (3%)
  starting transfers between devices  15.8 us (2%)
  between operations  15.5 us (2%)
    all_gather x2, waiting for transfers between devices, carried_in(): gathered = lax.all_gather(padded, axis).reshape(lax.axis_size(axis), -1)  136 us
    psum x1, blocking collectives, on_device(): grad_conv = lax.psum(weight_part, ('seq', 'head'))  95.7 us
    dynamic_update_slice x48, local copies, waits for them, and re-layouts, attention_grads(): forward_out = lax.scan(forward_block, (prefix[0], prefix[1]), indices)  55 us
    all_to_all x1, blocking collectives, on_device(): lax.all_to_all(grad_mixed, 'head', split_axis=0, concat_axis=1, tiled=True)  41 us
    all_to_all x1, waiting for transfers between devices, on_device(): lax.all_to_all(outgoing, 'head', split_axis=1, concat_axis=0, tiled=True)  32.9 us
    all_to_all x1, waiting for transfers between devices, on_device(): lax.all_to_all(out_grads, 'head', split_axis=1, concat_axis=0, tiled=True)  28.9 us
    unnamed x48, local copies, waits for them, and re-layouts  23.9 us
    scatter-add x2, other arithmetic, feature_map(): columns[:, upper_j, :]  21.3 us
  transfers between devices with their start and end apart: 6, of which 4 were waited for; matrix products, arithmetic and copies ran while one was open for 2% of the time, Pallas kernels for 0%

commit v1 on v0

--- a/solution.py
+++ b/solution.py
@@ -8,6 +8,12 @@
 KEY_DIM = 16
 HEAD_DIM = 128
 HIGHEST = lax.Precision.HIGHEST
+
+
+def summed_here(shard, mesh_axis):
+    terms = lax.all_gather(shard, mesh_axis, axis=0, tiled=False)
+    acc = terms.sum(axis=0)
+    return acc
 
 
 def segment_sum(gathered, flags, here, reverse):
@@ -243,7 +249,7 @@
     grad_projected, weight_part = conv_backward(
         returned, trailing, projected, leading, conv_weight, token_offsets
     )
-    grad_conv = lax.psum(weight_part, ("seq", "head"))
+    grad_conv = summed_here(weight_part, ("seq", "head"))
     return (grad_projected, grad_conv)
 
 

time: 743 us -> 784 us (1.055)
  waiting for transfers between devices: 198 us -> 318 us
  blocking collectives: 137 us -> 40.8 us
  other arithmetic: 85.8 us -> 99.4 us
    all_gather x0 -> x1, waiting for transfers between devices: none -> 121 us  [summed_here(): terms = lax.all_gather(shard, mesh_axis, axis=0, tiled=False)]
    psum x1 -> x0, blocking collectives: 95.7 us -> none  [on_device(): grad_conv = lax.psum(weight_part, ('seq', 'head'))]
    reduce_sum x0 -> x1, other arithmetic: none -> 12.6 us  [summed_here(): acc = terms.sum(axis=0)]
    unnamed x48 -> x70, local copies, waits for them, and re-layouts: 23.9 us -> 24.5 us
  transfers between devices with their start and end apart: 6 -> 7, of which waited for: 4 -> 6; matrix products, arithmetic and copies ran while one was open for 2% -> 3% of each run, Pallas kernels for 0% -> 0%
where the time goes in v1:
time: 784 us; the launch traced here: 773 us
  waiting for transfers between devices  318 us (41%)
  local copies, waits for them, and re-layouts  143 us (18%)
  matrix products  117 us (15%)
  other arithmetic  99.4 us (13%)
  blocking collectives  40.8 us (5%)
  loops' own time  23.5 us (3%)
  starting transfers between devices  16.4 us (2%)
  between operations  15.6 us (2%)
    all_gather x2, waiting for transfers between devices, carried_in(): gathered = lax.all_gather(padded, axis).reshape(lax.axis_size(axis), -1)  133 us
    all_gather x1, waiting for transfers between devices, summed_here(): terms = lax.all_gather(shard, mesh_axis, axis=0, tiled=False)  121 us
    dynamic_update_slice x48, local copies, waits for them, and re-layouts, attention_grads(): forward_out = lax.scan(forward_block, (prefix[0], prefix[1]), indices)  55.1 us
    all_to_all x1, blocking collectives, on_device(): lax.all_to_all(grad_mixed, 'head', split_axis=0, concat_axis=1, tiled=True)  40.8 us
    all_to_all x1, waiting for transfers between devices, on_device(): lax.all_to_all(outgoing, 'head', split_axis=1, concat_axis=0, tiled=True)  32.8 us
    all_to_all x1, waiting for transfers between devices, on_device(): lax.all_to_all(out_grads, 'head', split_axis=1, concat_axis=0, tiled=True)  29.1 us
    unnamed x70, local copies, waits for them, and re-layouts  24.5 us
    scatter-add x2, other arithmetic, feature_map(): columns[:, upper_j, :]  21.3 us
  transfers between devices with their start and end apart: 7, of which 6 were waited for; matrix products, arithmetic and copies ran while one was open for 3% of the time, Pallas kernels for 0%

profile of v1, /device:TPU:1, one launch (start us, length us, event | category | flops | bytes accessed | tf_op | source)
XLA Modules:
  0.0 773.1 jit_solution(16962347574090748644)
XLA Ops:
  8.1 4.0 collective-permute-start
  17.6 3.1 multiply_add_fusion.1
  20.7 6.1 all-to-all-start
  28.8 32.8 %all-to-all-done = f32[128,8,320]{0,2,1:T(8,128)S(1)} async-done(((f32[128,8,320]{0,2,1:T(8,128)}), f32[128,8,320]{0,2,1:T(8,128)S(1)}, u32[]{:S(2)}, u32[]{:S(2)}) %all-to-all-start) | async-done | bytes 1310752 | tf_op jit(solution)/shard_map/all_to_all | solution.py:242
  64.6 3.0 gather_fusion.1
  67.6 3.1 gather_fusion.2
  70.7 3.0 gather_fusion.3
  73.7 3.1 fusion.89
  76.8 4.2 fusion.98
  83.7 2.5 copy.231
  86.2 4.2 all-to-all-start.1
  90.5 29.1 %all-to-all-done.1 = f32[128,8,256]{0,2,1:T(8,128)} async-done(((f32[128,8,256]{0,2,1:T(8,128)}), f32[128,8,256]{0,2,1:T(8,128)}, u32[]{:S(2)}, u32[]{:S(2)}) %all-to-all-start.1) | async-done | bytes 1048608 | tf_op jit(solution)/shard_map/all_to_all | solution.py:243
  119.7 2.8 copy.232
  122.5 2.4 reshape.233
  127.7 2.5 copy.272
  130.2 45.0 %all-gather.6.cloned.1.call-done = f32[64,309,128]{2,1,0:T(8,128)} async-done(((f32[1,309,128]{2,1,0:T(8,128)}), f32[64,309,128]{2,1,0:T(8,128)}) %all-gather.6.cloned.1.call-update) | async-done | bytes 10125328 | tf_op jit(solution)/shard_map/all_gather | solution.py:38
  175.2 5.7 copy.306
  184.8 110.5 %while.46 = (s32[]{:T(128)}, f32[2,153,128]{2,1,0:T(8,128)S(1)}, f32[2,153]{1,0:T(2,128)S(1)}, f32[8,128,2,128]{1,0,3,2:T(8,128)}, f32[8,2,128]{2,1,0:T(2,128)S(...) while((s32[]{:T(128)}, f32[2,153,128]{2,1,0:T(8,128)S(1)}, ...), condition=%wide.region_10.11_spmd.clone, body=%wide.region_7.10_spmd.clone.sunk | while | flops 231664960 | bytes 3280461 | solution.py:156
  189.1 4.8 dynamic_update_slice.74
  202.9 4.8 dynamic_update_slice.74
  216.7 4.8 dynamic_update_slice.74
  230.5 4.8 dynamic_update_slice.74
  244.3 4.8 dynamic_update_slice.74
  258.1 4.8 dynamic_update_slice.74
  271.9 4.8 dynamic_update_slice.74
  285.6 4.8 dynamic_update_slice.74
  295.4 2.4 reshape.237
  302.3 2.8 fusion.81
  306.6 87.9 %all-gather.8.cloned.1.call-done = f32[64,309,128]{2,1,0:T(8,128)} async-done(((f32[1,309,128]{2,1,0:T(8,128)}), f32[64,309,128]{2,1,0:T(8,128)}) %all-gather.8.cloned.1.call-update) | async-done | bytes 10125328 | tf_op jit(solution)/shard_map/all_gather | solution.py:38
  394.6 5.7 copy.305
  404.9 114.0 %while.47 = (s32[]{:T(128)}, f32[2,153,128]{2,1,0:T(8,128)S(1)}, f32[2,153]{1,0:T(2,128)S(1)}, f32[8,2,153,128]{3,2,1,0:T(8,128)}, f32[8,2,153,128]{3,2,1,0:T(8,...) while((s32[]{:T(128)}, f32[2,153,128]{2,1,0:T(8,128)S(1)}, ...), condition=%wide.region_14.15_spmd.clone, body=%wide.region_13.14_spmd.clone.sunk | while | flops 462717824 | bytes 4866477 | solution.py:216
  412.1 2.0 fusion.190
  440.5 2.0 fusion.190
  483.2 2.0 fusion.190
  497.4 2.0 fusion.190
  518.8 2.0 copy.242
  527.4 6.0 fusion.85
  533.4 14.0 %scatter_fusion = f32[2,16,1024]{2,0,1:T(2,128)S(1)} fusion(f32[2,16,1024]{2,0,1:T(2,128)S(1)} %split.16, s32[136]{0:T(256)S(1)} %copy-done.21, f32[136,2,1024]{2,1,0:T(2,128)} %get-tuple-element.822), kind=kCustom, calls=%fused_computation.4 | custom fusion | flops 278528 | bytes 3342880 | tf_op jit(solution)/shard_map/transpose(jvp())/scatter-add | solution.py:55
  547.4 7.6 scatter_fusion.1
  556.2 7.6 scatter_fusion.3
  563.8 7.3 scatter_fusion.2
  572.6 2.7 pad_maximum_fusion
  576.9 40.8 %all_to_all.51 = f32[8,128,320]{1,2,0:T(8,128)S(1)} all-to-all(f32[8,128,320]{1,2,0:T(8,128)S(1)} %copy.248), channel_id=1, replica_groups=mesh['seq'=64,'head'=8] {'head'}, dimensions={0} | all-to-all | bytes 2621440 | tf_op jit(solution)/shard_map/all_to_all | solution.py:247
  617.8 2.2 multiply_reduce_fusion.2
  623.0 2.6 collective-permute-done.1
  627.1 4.4 fusion.75
  633.0 120.5 %all-gather.10.cloned.1.call-done = f32[512,3,2560]{2,1,0:T(4,128)} async-done(((f32[1,3,2560]{2,1,0:T(4,128)}), f32[512,3,2560]{2,1,0:T(4,128)}) %all-gather.10.cloned.1.call-update) | async-done | bytes 15728656 | tf_op jit(solution)/shard_map/all_gather | solution.py:14
  753.5 12.6 %reduce_sum.97 = f32[3,2560]{1,0:T(4,128)} reduce(f32[512,3,2560]{2,1,0:T(4,128)} %all-gather.10.cloned.1.call-done, f32[]{:T(128)} %constant.143.clone.1), dimensions={0}, to_apply=%region_22.23 | reduce | flops 3924480 | bytes 15759364 | tf_op jit(solution)/shard_map/reduce_sum | solution.py:15
  (438 shorter events, 202.1 us)
Async XLA Ops:
  8.1 9.1 %collective-permute-start = (f32[2,2560]{1,0:T(2,128)S(1)}, f32[2,2560]{1,0:T(2,128)S(1)}, u32[]{:S(2)}, u32[]{:S(2)}) collective-permute-start(f32[2,2560]{1,0:T(2,128)S(1)} %slice.116), channel_id=1, source_target_pairs={{0,1},{1,2},{2,3},{3,4},{4,5},{5,6},{6,7},{7,8},{8,9},{9,10},{10,1... | collective-permute-start | bytes 61448 | tf_op jit(solution)/shard_map/ppermute | solution.py:48
  14.4 3.2 copy-start.23
  14.4 3.2 copy-start.25
  15.4 2.2 copy-start.14
  15.4 2.2 copy-start.16
  15.4 2.2 copy-start.18
  17.1 3.6 copy-start.3
  17.6 3.1 copy-start.5
  20.7 7.4 copy-start.22
  20.7 7.4 copy-start.21
  20.7 40.9 %all-to-all-start = ((f32[128,8,320]{0,2,1:T(8,128)}), f32[128,8,320]{0,2,1:T(8,128)S(1)}, u32[]{:S(2)}, u32[]{:S(2)}) async-start(f32[128,8,320]{0,2,1:T(8,128)} %bitcast.250), calls=%async_computation | async-start | bytes 2621440 | tf_op jit(solution)/shard_map/all_to_all | solution.py:242
  26.8 148.4 %all-gather.6.cloned.1.call-start = ((), (), s32[]{:S(2)}) async-start(), calls=%async_computation.3 | async-start | bytes 10383360 | tf_op jit(solution)/shard_map/all_gather | solution.py:38
  27.0 63.5 %copy-start.20 = (s32[1026]{0:T(1024)}, s32[1026]{0:T(1024)S(1)}, u32[]{:S(2)}) copy-start(s32[1026]{0:T(1024)S(1)} %select_reduce_fusion) | copy-start | bytes 12316
  64.6 9.1 %copy-start.7 = (f32[136,2,1024]{2,1,0:T(2,128)}, f32[136,2,1024]{2,1,0:T(2,128)S(1)}, u32[]{:S(2)}) copy-start(f32[136,2,1024]{2,1,0:T(2,128)S(1)} %gather_fusion) | copy-start | bytes 3342340
  70.7 3.0 copy-start.27
  86.2 33.5 %all-to-all-start.1 = ((f32[128,8,256]{0,2,1:T(8,128)}), f32[128,8,256]{0,2,1:T(8,128)}, u32[]{:S(2)}, u32[]{:S(2)}) async-start(f32[128,8,256]{0,2,1:T(8,128)} %bitcast.257), calls=%async_computation.1 | async-start | bytes 2097152 | tf_op jit(solution)/shard_map/all_to_all | solution.py:243
  90.5 304.1 %all-gather.8.cloned.1.call-start = ((), (), s32[]{:S(2)}) async-start(), calls=%async_computation.4 | async-start | bytes 10383360 | tf_op jit(solution)/shard_map/all_gather | solution.py:38
  125.9 1.3 copy-start.10
  183.5 1.3 slice-start.1
  297.7 2.9 copy-start.2
  299.6 1.0 copy-start
  305.9 447.6 %all-gather.10.cloned.1.call-start = ((), (), s32[]{:S(2)}) async-start(), calls=%async_computation.5 | async-start | bytes 21012480 | tf_op jit(solution)/shard_map/all_gather | solution.py:14
  520.9 1.7 copy-start.9
  524.3 3.1 copy-start.8
  526.3 7.0 copy-start.1
  533.4 14.0 %copy-start.13 = (f32[136,2,1024]{2,1,0:T(2,128)S(1)}, f32[136,2,1024]{2,1,0:T(2,128)}, u32[]{:S(2)}) copy-start(f32[136,2,1024]{2,1,0:T(2,128)} %get-tuple-element.821) | copy-start | bytes 3342340
  555.0 1.2 copy-start.12
  556.2 7.6 slice-start
  556.2 7.6 copy-start.11
  576.6 41.1 %copy-start.24 = (f32[128]{0:T(128)S(1)}, f32[128]{0:T(128)}, u32[]{:S(2)}) copy-start(f32[128]{0:T(128)} %copy-done.23) | copy-start | bytes 1540
  576.6 41.1 %copy-start.26 = (f32[128]{0:T(128)S(1)}, f32[128]{0:T(128)}, u32[]{:S(2)}) copy-start(f32[128]{0:T(128)} %copy-done.25) | copy-start | bytes 1540
  576.9 40.8 %copy-start.4 = (f32[128,2560]{0,1:T(8,128)S(1)}, f32[128,2560]{0,1:T(8,128)}, u32[]{:S(2)}) copy-start(f32[128,2560]{0,1:T(8,128)} %copy-done.3) | copy-start | bytes 3932164
  576.9 40.8 %copy-start.6 = (f32[2,2560]{0,1:T(8,128)S(1)}, f32[2,2560]{0,1:T(8,128)}, u32[]{:S(2)}) copy-start(f32[2,2560]{0,1:T(8,128)} %copy-done.5) | copy-start | bytes 61444
  620.6 6.5 copy-start.15
  620.7 6.5 copy-start.17
  620.7 6.5 copy-start.19
  620.7 6.5 copy-start.28
  620.7 6.5 copy-start.29
  621.1 4.5 collective-permute-start.1
Sparse Core Ops, SparseCore 0:
  83.8 91.4 all-gather.5
  306.0 88.5 all-gather.7
  620.8 132.6 all-gather.9
